TPU v7x, 32 devices: a whole 2x2x4 slice. The times are simulated.
32 devices in a mesh: groups: 2 (over y), paths: 4 (over z), cols: 2 (over x), depth: 2 (over core).
Axes of the slice: x: 2, y: 2, z: 4, core: 2. Of those that a mesh axis runs over, the one named last changes fastest.
Arguments:
- panels: bfloat16 [96, 64, 1024], P(('groups', 'cols', 'paths'), None, 'depth'), parts along dimension 0, may hold values from -0.0546875 to 0.0546875
- model: bfloat16 [96, 1024], P(('groups', 'cols', 'paths'), 'depth'), parts along dimension 0, may hold values from -6 to 6
- depth_weight: bfloat16 [2048, 1024], P(('groups', 'paths'), 'depth'), parts along dimension 0, may hold values from -6 to 6
- seg_len: bfloat16 [2048, 48], P(('groups', 'paths'), 'cols'), parts along dimension 0, may hold values from 0.29882812 to 3
- path_start: int32 [2048], P(('groups', 'paths')), parts along dimension 0, may hold values from 0 to 47, as said below
- path_end: int32 [2048], P(('groups', 'paths')), parts along dimension 0, may hold values from 1 to 48, as said below
- mode_index: int32 [2048, 4], P(('groups', 'paths')), parts along dimension 0, may hold values from 0 to 63, all different within a row
- observed: float32 [2048, 4], P(('groups', 'paths')), parts along dimension 0, may hold values from -6 to 6
Outputs:
- gradient: float32 [96, 1024], P(('groups', 'cols', 'paths'), 'depth'), parts along dimension 0
- misfit: float32 [2048, 4], P(('groups', 'paths')), parts along dimension 0
There are 2 independent parts, one for each index of `groups`. A program takes and returns all parts, laid end to end along the dimension named above; each array names one. Nothing has to cross between parts.
Inputs may be any that keep to these rules, and one draw needn't show every extreme that they name: `path_start`: each path starts before it ends; path 0 spans all 48 columns. `path_end`: each path ends after it starts. `mode_index`: each path names 4 different modes.
All inputs are finite; a program needn't handle non-finite values.
Results may differ from a plain program's by a relative error of at most 0.011.
Values may be sent and summed in bfloat16 or wider, within the bound.
No kernel may reach another device: no remote copies, remote signals or barrier semaphores. Data moves between devices by JAX's collectives and lax.ppermute only.
A program may use at most 64 MiB of HBM per device.

v0:
```python
import jax
import jax.numpy as jnp
from jax import lax
from jax.sharding import PartitionSpec as P


def finish(partial_value, one_hot, observed):
    combined = lax.psum(partial_value, ("cols", "depth"))
    travel = jnp.einsum("pkm,pm->pk", one_hot, combined)
    misfit = travel - observed
    resid_modes = jnp.einsum("pk,pkm->pm", misfit, one_hot)
    return (misfit, resid_modes)


def shards(panels, model, depth_weight, seg_len, path_start, path_end, mode_index, observed):
    own_cols, modes, depth_half = panels.shape
    path_rows, block_cols = seg_len.shape
    columns = lax.axis_index("cols") * block_cols + lax.iota(jnp.int32, block_cols)
    inside = (columns[None, :] >= path_start[:, None]) & (columns[None, :] < path_end[:, None])
    lengths = jnp.where(inside, seg_len, jnp.zeros_like(seg_len))
    one_hot = (mode_index[:, :, None] == lax.iota(jnp.int32, modes)[None, None, :]).astype(
        jnp.float32
    )
    kernel_piece = lax.all_gather(panels, "paths", axis=0, tiled=True)
    model_piece = lax.all_gather(model, "paths", axis=0, tiled=True)
    row_count = kernel_piece.shape[0]
    scaled = (
        kernel_piece.astype(jnp.float32) * model_piece.astype(jnp.float32)[:, None, :]
    ).astype(jnp.bfloat16)
    scaled = scaled.reshape(row_count * modes, depth_half)
    weighted = lax.dot_general(
        depth_weight, scaled, (((1,), (1,)), ((), ())), preferred_element_type=jnp.float32
    )
    weighted = weighted.reshape(path_rows, row_count, modes)
    row_weights = lengths.astype(jnp.float32)
    partial_value = jnp.einsum("pc,pcm->pm", row_weights, weighted)
    misfit, resid_modes = finish(partial_value, one_hot, observed)
    kernel_piece = lax.all_gather(panels, "paths", axis=0, tiled=True)
    row_count = kernel_piece.shape[0]
    row_weights = lengths.astype(jnp.float32)
    spread = (
        (row_weights[:, :, None] * resid_modes[:, None, :])
        .astype(jnp.bfloat16)
        .reshape(path_rows, row_count * modes)
    )
    summed = lax.dot_general(
        spread, depth_weight, (((0,), (0,)), ((), ())), preferred_element_type=jnp.float32
    )
    summed = summed.reshape(row_count, modes, depth_half)
    block_terms = jnp.sum(summed * kernel_piece.astype(jnp.float32), axis=1)
    gradient = lax.psum_scatter(block_terms, "paths", scatter_dimension=0, tiled=True)
    return (gradient, misfit)


def solution(mesh):
    return jax.shard_map(
        shards,
        mesh=mesh,
        in_specs=(
            P(("groups", "cols", "paths"), None, "depth"),
            P(("groups", "cols", "paths"), "depth"),
            P(("groups", "paths"), "depth"),
            P(("groups", "paths"), "cols"),
            P(("groups", "paths")),
            P(("groups", "paths")),
            P(("groups", "paths"), None),
            P(("groups", "paths"), None),
        ),
        out_specs=(P(("groups", "cols", "paths"), "depth"), P(("groups", "paths"), None)),
        check_vma=False,
    )
```

profile of v0, /device:TPU:0, one launch (start us, length us, event | category | flops | bytes accessed | tf_op | source)
XLA Modules:
  0.0 111.6 jit_solution(14641012471253387348)
XLA Ops:
  7.2 0.0 copy-start
  7.2 0.0 all-gather.3.cloned.1.call-start
  7.2 0.7 all-gather.3.cloned.1.call-update
  7.9 0.0 all-reduce.4.cloned.1.call-start
  8.0 15.0 %all-gather = bf16[4,6,512]{2,1,0:T(8,128)(2,1)S(1)} all-gather(bf16[1,6,512]{2,1,0:T(8,128)(2,1)} %bitcast.28), channel_id=1, replica_groups=mesh['groups'=2,'paths'=4,'cols'=2,'depth'=2] {'paths'}, dimensions={0}, use_global_device_ids=true | all-gather | bytes 30720 | tf_op jit(solution)/shard_map/all_gather | solution.py:25
  23.0 0.8 fusion.10
  23.8 25.6 %all-gather.3.cloned.1.call-done = bf16[24,64,512]{2,1,0:T(8,128)(2,1)} async-done(((bf16[6,64,512]{2,1,0:T(8,128)(2,1)}), bf16[24,64,512]{2,1,0:T(8,128)(2,1)}) %all-gather.3.cloned.1.call-update) | async-done | bytes 1572880 | tf_op jit(solution)/shard_map/all_gather | solution.py:24
  49.4 1.7 %fusion.1 = bf16[24,64,512]{2,1,0:T(8,128)(2,1)S(1)} fusion(bf16[24,64,512]{2,1,0:T(8,128)(2,1)} %all-gather.3.cloned.1.call-done, f32[24,512]{1,0:T(8,128)S(1)} %reshape.31), kind=kLoop, calls=%fused_computation.2 | loop fusion | flops 2359296 | bytes 3194880 | tf_op jit(solution)/shard_map/convert_element_type | solution.py:29
  51.2 0.0 copy-done
  51.2 0.6 fusion.11
  51.8 0.0 copy-start.3
  51.8 0.1 multiply_reduce_fusion
  51.9 0.0 copy-start.4
  52.0 0.8 copy.17
  52.7 0.0 all-reduce.4.cloned.1.call-update
  52.7 0.0 copy-done.3
  52.7 0.1 copy.12
  52.9 30.3 %all-reduce.4.cloned.1.call-done = f32[256,64]{1,0:T(8,128)} async-done(((f32[256,64]{1,0:T(8,128)}), f32[256,64]{1,0:T(8,128)}) %all-reduce.4.cloned.1.call-update) | async-done | bytes 65552 | tf_op jit(solution)/shard_map/psum | solution.py:8
  83.2 1.4 %fusion.7 = f32[256,1,4]{2,1,0:T(1,128)S(1)} fusion(f32[256,64,1]{1,2,0:T(1,128)} %bitcast.29, s32[256,4]{1,0:T(8,128)S(1)} %copy.12), kind=kOutput, calls=%fused_computation.11 | convolution fusion | flops 196608 | bytes 73728 | tf_op jit(solution)/shard_map/pkm,pm->pk/dot_general | solution.py:9
  84.6 0.1 copy.19
  84.7 0.0 copy-start.2
  84.7 0.1 copy.26
  84.8 1.4 %select_reduce_fusion = f32[256,64]{1,0:T(8,128)S(1)} fusion(f32[256,4]{1,0:T(8,128)S(1)} %copy.26, s32[256,4]{1,0:T(8,128)S(1)} %copy.12), kind=kLoop, calls=%fused_computation.9 | loop fusion | flops 180224 | bytes 73728
  86.3 0.1 copy.23
  86.4 0.0 copy-start.5
  86.4 0.6 fusion.2
  87.0 12.8 %fusion = f32[8,512]{1,0:T(8,128)S(1)} fusion(f32[24,512]{1,0:T(8,128)S(1)} %fusion.2), kind=kCustom, calls=%all-reduce-scatter | all-reduce-scatter fusion | flops 16385 | bytes 66048
  99.8 2.9 %collective-permute-start = (f32[6,512]{1,0:T(8,128)S(1)}, f32[6,512]{1,0:T(8,128)S(1)}, u32[]{:S(2)}, u32[]{:S(2)}) collective-permute-start(f32[6,512]{1,0:T(8,128)S(1)} %slice), channel_id=1, source_target_pairs={{0,4},{4,8},{8,12},{1,5},{5,9},{9,13},{2,6},{6,10},{10,14},{3,7},{... | collective-permute-start | bytes 36872
  102.7 0.6 dynamic-slice.4
  103.9 0.2 collective-permute-done
  104.1 0.1 concatenate
  104.2 0.6 constant_dynamic-slice_fusion
  (9 shorter events, 0.0 us)
Async XLA Ops:
  7.2 44.0 %copy-start = (bf16[256,512]{1,0:T(8,128)(2,1)S(1)}, bf16[256,512]{1,0:T(8,128)(2,1)}, u32[]{:S(2)}) copy-start(bf16[256,512]{1,0:T(8,128)(2,1)} %param.10) | copy-start | bytes 786436
  7.2 42.2 %all-gather.3.cloned.1.call-start = ((), (), s32[]{:S(2)}) async-start(), calls=%async_computation | async-start | bytes 1966080 | tf_op jit(solution)/shard_map/all_gather | solution.py:24
  7.9 75.2 %all-reduce.4.cloned.1.call-start = ((), (), s32[]{:S(2)}) async-start(), calls=%async_computation.1 | async-start | bytes 262144 | tf_op jit(solution)/shard_map/psum | solution.py:8
  51.8 1.0 copy-start.3
  51.9 32.7 %copy-start.4 = (f32[256,4]{0,1:T(4,128)S(1)}, f32[256,4]{0,1:T(4,128)}, u32[]{:S(2)}) copy-start(f32[256,4]{0,1:T(4,128)} %param.15) | copy-start | bytes 12292
  52.7 33.7 %copy-start.1 = (bf16[24,64,512]{2,1,0:T(8,128)(2,1)S(1)}, bf16[24,64,512]{2,1,0:T(8,128)(2,1)}, u32[]{:S(2)}) copy-start(bf16[24,64,512]{2,1,0:T(8,128)(2,1)} %all-gather.3.cloned.1.call-done) | copy-start | bytes 4718596
  84.7 2.3 %copy-start.2 = (f32[256,4]{0,1:T(4,128)}, f32[256,4]{0,1:T(4,128)S(1)}, u32[]{:S(2)}) copy-start(f32[256,4]{0,1:T(4,128)S(1)} %bitcast_subtract_fusion) | copy-start | bytes 12292
  86.4 16.3 %copy-start.5 = (u32[32]{0:T(128)S(1)}, u32[32]{0:T(128)}, u32[]{:S(2)}) copy-start(u32[32]{0:T(128)} %constant.17) | copy-start | bytes 388
  99.8 4.3 %collective-permute-start = (f32[6,512]{1,0:T(8,128)S(1)}, f32[6,512]{1,0:T(8,128)S(1)}, u32[]{:S(2)}, u32[]{:S(2)}) collective-permute-start(f32[6,512]{1,0:T(8,128)S(1)} %slice), channel_id=1, source_target_pairs={{0,4},{4,8},{8,12},{1,5},{5,9},{9,13},{2,6},{6,10},{10,14},{3,7},{... | collective-permute-start | bytes 36872
Sparse Core Ops, SparseCore 0:
  9.6 39.7 all-gather.2
  52.9 30.2 all-reduce.3
where the time goes:
time: 112 us
  waiting for transfers between devices  56.8 us (51%)
  blocking collectives  27.8 us (25%)
  between operations  14.9 us (13%)
  other arithmetic  4.14 us (4%)
  starting transfers between devices  2.94 us (3%)
  matrix products  2.64 us (2%)
  local copies, waits for them, and re-layouts  2.5 us (2%)
    psum x1, waiting for transfers between devices, finish(): combined = lax.psum(partial_value, ('cols', 'depth'))  30.3 us
    all_gather x1, waiting for transfers between devices, shards(): kernel_piece = lax.all_gather(panels, 'paths', axis=0, tiled=True)  25.6 us
    all_gather x1, blocking collectives, shards(): model_piece = lax.all_gather(model, 'paths', axis=0, tiled=True)  15 us
    unnamed x1, blocking collectives  12.8 us
    unnamed x1, starting transfers between devices  2.87 us
  transfers between devices with their start and end apart: 3, of which 3 were waited for; matrix products, arithmetic and copies ran while one was open for 1% of the time, Pallas kernels for 0%

commit v1 on v0

--- a/solution.py
+++ b/solution.py
@@ -5,7 +5,7 @@
 
 
 def finish(partial_value, one_hot, observed):
-    combined = lax.psum(partial_value, ("cols", "depth"))
+    combined = jnp.sum(lax.all_gather(partial_value, ("cols", "depth")), axis=0)
     travel = jnp.einsum("pkm,pm->pk", one_hot, combined)
     misfit = travel - observed
     resid_modes = jnp.einsum("pk,pkm->pm", misfit, one_hot)

time: 112 us -> 84.8 us (0.76)
  waiting for transfers between devices: 56.8 us -> 25.7 us
  blocking collectives: 27.8 us -> 33.2 us
  matrix products: 2.64 us -> 1.23 us
  starting transfers between devices: 2.94 us -> 1.7 us
    psum x1 -> x0, waiting for transfers between devices: 30.3 us -> none  [finish(): combined = lax.psum(partial_value, ('cols', 'depth'))]
    all_gather x0 -> x1, blocking collectives: none -> 5.92 us  [finish(): combined = jnp.sum(lax.all_gather(partial_value, ('cols', 'depth')), axis=0)]
    dot_general x1 -> x0, matrix products: 1.42 us -> none  [finish(): travel = jnp.einsum('pkm,pm->pk', one_hot, combined)]
    unnamed x1, starting transfers between devices: 2.87 us -> 1.66 us
    unnamed x18 -> x17, local copies, waits for them, and re-layouts: 1.58 us -> 2.35 us
  transfers between devices with their start and end apart: 3 -> 2, of which waited for: 3 -> 2; matrix products, arithmetic and copies ran while one was open for 1% -> 3% of each run, Pallas kernels for 0% -> 0%
where the time goes in v1:
time: 84.8 us; the launch traced here: 84.5 us
  blocking collectives  33.2 us (39%)
  waiting for transfers between devices  25.7 us (30%)
  between operations  14.9 us (18%)
  other arithmetic  5.19 us (6%)
  local copies, waits for them, and re-layouts  2.64 us (3%)
  starting transfers between devices  1.7 us (2%)
  matrix products  1.23 us (1%)
    all_gather x1, waiting for transfers between devices, shards(): kernel_piece = lax.all_gather(panels, 'paths', axis=0, tiled=True)  24.8 us
    all_gather x1, blocking collectives, shards(): model_piece = lax.all_gather(model, 'paths', axis=0, tiled=True)  15 us
    unnamed x1, blocking collectives  12.3 us
    all_gather x1, blocking collectives, finish(): combined = jnp.sum(lax.all_gather(partial_value, ('cols', 'depth')), axis=0)  5.92 us
    unnamed x17, local copies, waits for them, and re-layouts  2.35 us
    unnamed x2, other arithmetic  2.34 us
    convert_element_type x1, other arithmetic, shards(): scaled = (kernel_piece.astype(jnp.float32) * model_piece.astype(jnp.float...  1.74 us
  transfers between devices with their start and end apart: 2, of which 2 were waited for; matrix products, arithmetic and copies ran while one was open for 3% of the time, Pallas kernels for 0%

profile of v1, /device:TPU:0, one launch (start us, length us, event | category | flops | bytes accessed | tf_op | source)
XLA Modules:
  0.0 84.5 jit_solution(5725507183063496644)
XLA Ops:
  7.2 0.0 copy-start
  7.2 0.0 all-gather.4.cloned.1.call-start
  7.2 0.7 all-gather.4.cloned.1.call-update
  7.9 15.0 %all-gather.1 = bf16[4,6,512]{2,1,0:T(8,128)(2,1)S(1)} all-gather(bf16[1,6,512]{2,1,0:T(8,128)(2,1)} %bitcast.28), channel_id=1, replica_groups=mesh['groups'=2,'paths'=4,'cols'=2,'depth'=2] {'paths'}, dimensions={0}, use_global_device_ids=true | all-gather | bytes 30720 | tf_op jit(solution)/shard_map/all_gather | solution.py:25
  23.0 0.8 copy.14
  23.8 0.8 fusion.9
  24.6 24.8 %all-gather.4.cloned.1.call-done = bf16[24,64,512]{2,1,0:T(8,128)(2,1)} async-done(((bf16[6,64,512]{2,1,0:T(8,128)(2,1)}), bf16[24,64,512]{2,1,0:T(8,128)(2,1)}) %all-gather.4.cloned.1.call-update) | async-done | bytes 1572880 | tf_op jit(solution)/shard_map/all_gather | solution.py:24
  49.4 1.7 %fusion.1 = bf16[24,64,512]{2,1,0:T(8,128)(2,1)S(1)} fusion(bf16[24,64,512]{2,1,0:T(8,128)(2,1)} %all-gather.4.cloned.1.call-done, f32[24,512]{1,0:T(8,128)S(1)} %reshape.32), kind=kLoop, calls=%fused_computation.2 | loop fusion | flops 2359296 | bytes 3194880 | tf_op jit(solution)/shard_map/convert_element_type | solution.py:29
  51.2 0.0 copy-done
  51.2 0.6 fusion.10
  51.8 0.0 copy-start.3
  51.8 0.1 multiply_reduce_fusion
  51.9 0.0 copy-start.1
  52.0 5.9 %all-gather = f32[1024,64]{0,1:T(8,128)S(1)} all-gather(f32[256,64]{0,1:T(8,128)S(1)} %multiply_reduce_fusion), channel_id=2, replica_groups=mesh['groups'=2,'paths'=4,'cols'=2,'depth'=2] {'cols','depth'}, dimensions={0}, use_global_device_ids=true | all-gather | bytes 327680 | tf_op jit(solution)/shard_map/all_gather | solution.py:8
  57.9 0.1 reshape.29
  58.0 0.2 reduce_sum.18
  58.2 0.1 copy.31
  58.3 0.9 %select_reduce_fusion.1 = f32[256,4]{1,0:T(8,128)S(1)} fusion(f32[256,64]{1,0:T(8,128)S(1)} %copy.31, s32[256,4]{1,0:T(8,128)S(1)} %copy.14), kind=kLoop, calls=%fused_computation.10 | loop fusion | flops 195584 | bytes 73728
  59.2 0.1 copy.24
  59.2 0.0 copy-start.2
  59.3 0.1 copy.33
  59.4 1.4 %select_reduce_fusion = f32[256,64]{1,0:T(8,128)S(1)} fusion(f32[256,4]{1,0:T(8,128)S(1)} %copy.33, s32[256,4]{1,0:T(8,128)S(1)} %copy.14), kind=kLoop, calls=%fused_computation.9 | loop fusion | flops 180224 | bytes 73728
  60.9 0.1 copy.28
  60.9 0.0 copy-start.4
  61.0 0.6 fusion.2
  61.6 0.0 copy-done.2
  61.6 12.3 %fusion = f32[8,512]{1,0:T(8,128)S(1)} fusion(f32[24,512]{1,0:T(8,128)S(1)} %fusion.2), kind=kCustom, calls=%all-reduce-scatter | all-reduce-scatter fusion | flops 16385 | bytes 66048
  73.9 1.7 %collective-permute-start = (f32[6,512]{1,0:T(8,128)S(1)}, f32[6,512]{1,0:T(8,128)S(1)}, u32[]{:S(2)}, u32[]{:S(2)}) collective-permute-start(f32[6,512]{1,0:T(8,128)S(1)} %slice), channel_id=1, source_target_pairs={{0,4},{4,8},{8,12},{1,5},{5,9},{9,13},{2,6},{6,10},{10,14},{3,7},{... | collective-permute-start | bytes 36872
  75.6 0.6 dynamic-slice.4
  76.8 0.2 collective-permute-done
  77.0 0.1 concatenate
  77.1 0.6 constant_dynamic-slice_fusion
  (7 shorter events, 0.0 us)
Async XLA Ops:
  7.2 44.0 %copy-start = (bf16[256,512]{1,0:T(8,128)(2,1)S(1)}, bf16[256,512]{1,0:T(8,128)(2,1)}, u32[]{:S(2)}) copy-start(bf16[256,512]{1,0:T(8,128)(2,1)} %param.10) | copy-start | bytes 786436
  7.2 42.2 %all-gather.4.cloned.1.call-start = ((), (), s32[]{:S(2)}) async-start(), calls=%async_computation | async-start | bytes 1966080 | tf_op jit(solution)/shard_map/all_gather | solution.py:24
  51.8 7.5 %copy-start.3 = (f32[256,4]{0,1:T(4,128)S(1)}, f32[256,4]{0,1:T(4,128)}, u32[]{:S(2)}) copy-start(f32[256,4]{0,1:T(4,128)} %param.15) | copy-start | bytes 12292
  51.9 9.0 %copy-start.1 = (bf16[24,64,512]{2,1,0:T(8,128)(2,1)S(1)}, bf16[24,64,512]{2,1,0:T(8,128)(2,1)}, u32[]{:S(2)}) copy-start(bf16[24,64,512]{2,1,0:T(8,128)(2,1)} %all-gather.4.cloned.1.call-done) | copy-start | bytes 4718596
  59.2 2.4 %copy-start.2 = (f32[256,4]{0,1:T(4,128)}, f32[256,4]{0,1:T(4,128)S(1)}, u32[]{:S(2)}) copy-start(f32[256,4]{0,1:T(4,128)S(1)} %sub.3) | copy-start | bytes 12292
  60.9 14.6 %copy-start.4 = (u32[32]{0:T(128)S(1)}, u32[32]{0:T(128)}, u32[]{:S(2)}) copy-start(u32[32]{0:T(128)} %constant.19) | copy-start | bytes 388
  73.9 3.1 %collective-permute-start = (f32[6,512]{1,0:T(8,128)S(1)}, f32[6,512]{1,0:T(8,128)S(1)}, u32[]{:S(2)}, u32[]{:S(2)}) collective-permute-start(f32[6,512]{1,0:T(8,128)S(1)} %slice), channel_id=1, source_target_pairs={{0,4},{4,8},{8,12},{1,5},{5,9},{9,13},{2,6},{6,10},{10,14},{3,7},{... | collective-permute-start | bytes 36872
Sparse Core Ops, SparseCore 0:
  9.6 39.7 all-gather.3
